TPU v7x, 512 devices: a whole 4x4x16 slice. The times are simulated.
512 devices in a mesh: head: 4 (over x_lo, core), seq: 128 (over x_hi, z, y).
Axes of the slice: x: 4 (x_hi: 2, x_lo: 2; x = x_hi * 2 + x_lo), y: 4, z: 16, core: 2. Of those that a mesh axis runs over, the one named last changes fastest.
Arguments:
- queries: bfloat16 [32768, 32, 128], P('seq', 'head'), may hold values from -6 to 6
- normed_keys: bfloat16 [32768, 16, 128], P('seq', 'head'), may hold values from -6 to 6
- value_matrix: bfloat16 [32768, 16, 128], P('seq', 'head'), may hold values from -6 to 6
- forward_out: bfloat16 [32768, 32, 128], P('seq', 'head'), may hold values from -1.75 to 1.75
- output_gradient: bfloat16 [32768, 32, 128], P(('seq', 'head')), may hold values from -96 to 96
- row_log_total: float32 [32, 32768], P('head', 'seq'), may hold values from 6 to 8
- pair_start: int32 [32768], P('seq'), may hold values from 0 to 32256, as said below
Outputs:
- query_grad: bfloat16 [32768, 32, 128], P(('seq', 'head'))
- key_grad: bfloat16 [32768, 16, 128], P(('seq', 'head'))
- value_grad: bfloat16 [32768, 16, 128], P(('seq', 'head'))
Inputs may be any that keep to these rules, and one draw needn't show every extreme that they name: pair_start[p] is the first position of the pair that holds token p: it never falls, never exceeds p, and equals p at each pair's first token; the last pair holds the final 1024 / 2 tokens, the pair before it at most 1024 tokens, and every other pair 1024 / 8 to 1024 tokens.
All inputs are finite; a program needn't handle non-finite values.
Results may differ from a plain program's by a relative error of at most 0.0059.
Values may be sent and summed in bfloat16 or wider, within the bound.
No kernel may reach another device: no remote copies, remote signals or barrier semaphores. Data moves between devices by JAX's collectives and lax.ppermute only.
A program may use at most 64 MiB of HBM per device.

v0:
```python
import jax
import jax.numpy as jnp
from jax import lax
from jax.sharding import Mesh
from jax.sharding import PartitionSpec as P

WINDOW_LENGTH = 1024
BLOCK = 256
score_scale = 168.0 ** (-0.5)


def shifted(value, axis, by):
    size = lax.axis_size(axis)
    pairs = [(i, i + by) for i in range(size) if 0 <= i + by < size]
    return lax.ppermute(value, axis, pairs)


def band_terms(query, grad, logsum, delta, start, base, keys, values):
    tokens, group, depth = query.shape
    tiles = tokens // BLOCK
    span = WINDOW_LENGTH + BLOCK
    query_t = query.reshape(tiles, BLOCK, group, depth)
    grad_t = grad.reshape(tiles, BLOCK, group, depth)
    logsum_t = logsum.reshape(group, tiles, BLOCK).transpose(1, 0, 2)
    delta_t = delta.reshape(group, tiles, BLOCK).transpose(1, 0, 2)
    start_t = start.reshape(tiles, BLOCK)
    key_w = jnp.stack([keys[t * BLOCK : t * BLOCK + span] for t in range(tiles)])
    value_w = jnp.stack([values[t * BLOCK : t * BLOCK + span] for t in range(tiles)])
    tile_base = base + BLOCK * jnp.arange(tiles, dtype=jnp.int32)
    query_place = tile_base[:, None] + jnp.arange(BLOCK, dtype=jnp.int32)[None, :]
    key_place = tile_base[:, None] - WINDOW_LENGTH + jnp.arange(span, dtype=jnp.int32)[None, :]
    gap = query_place[:, :, None] - key_place[:, None, :]
    visible = (gap >= 0) & (gap < WINDOW_LENGTH) & (key_place[:, None, :] >= start_t[:, :, None])
    scores = (
        jnp.einsum("tigd,tjd->tgij", query_t, key_w, preferred_element_type=jnp.float32)
        * score_scale
    )
    probs = jnp.where(visible[:, None], jnp.exp(scores - logsum_t[..., None]), 0.0)
    dprobs = jnp.einsum("tigd,tjd->tgij", grad_t, value_w, preferred_element_type=jnp.float32)
    low_scores = (probs * (dprobs - delta_t[..., None])).astype(jnp.bfloat16)
    low_probs = probs.astype(jnp.bfloat16)
    query_term = jnp.einsum("tgij,tjd->tigd", low_scores, key_w, preferred_element_type=jnp.float32)
    key_w_term = jnp.einsum(
        "tgij,tigd->tjd", low_scores, query_t, preferred_element_type=jnp.float32
    )
    value_w_term = jnp.einsum(
        "tgij,tigd->tjd", low_probs, grad_t, preferred_element_type=jnp.float32
    )
    total = WINDOW_LENGTH + tokens
    key_term = jnp.zeros((total, depth), jnp.float32)
    value_term = jnp.zeros((total, depth), jnp.float32)
    for t in range(tiles):
        key_term = key_term.at[t * BLOCK : t * BLOCK + span].add(key_w_term[t])
        value_term = value_term.at[t * BLOCK : t * BLOCK + span].add(value_w_term[t])
    return (query_term.reshape(tokens, group, depth), key_term, value_term)


def on_device(
    queries, normed_keys, value_matrix, forward_out, output_gradient, row_log_total, pair_start
):
    grad_rows = lax.all_to_all(output_gradient, "head", split_axis=1, concat_axis=0, tiled=True)
    delta_rows = jnp.einsum(
        "thd,thd->ht", forward_out, grad_rows, preferred_element_type=jnp.float32
    )
    ring = lax.axis_size("sl")
    query_g = lax.all_to_all(queries, "sl", split_axis=1, concat_axis=0, tiled=True)
    grad_g = lax.all_to_all(grad_rows, "sl", split_axis=1, concat_axis=0, tiled=True)
    key_g = lax.all_to_all(normed_keys, "sl", split_axis=1, concat_axis=0, tiled=True)
    value_g = lax.all_to_all(value_matrix, "sl", split_axis=1, concat_axis=0, tiled=True)
    logsum_g = lax.all_to_all(row_log_total, "sl", split_axis=0, concat_axis=1, tiled=True)
    delta_g = lax.all_to_all(delta_rows, "sl", split_axis=0, concat_axis=1, tiled=True)
    start_g = lax.all_gather(pair_start, "sl", axis=0, tiled=True)
    tokens, group, depth = query_g.shape
    base = lax.axis_index("sh") * tokens
    key_own = key_g[:, 0]
    value_own = value_g[:, 0]
    key_far = shifted(key_own, "sh", 1)
    value_far = shifted(value_own, "sh", 1)
    keys = jnp.concatenate([key_far, key_own], axis=0)
    values = jnp.concatenate([value_far, value_own], axis=0)
    query_sum, key_sum, value_sum = band_terms(
        query_g, grad_g, logsum_g, delta_g, start_g, base, keys, values
    )
    key_back = shifted(key_sum[:WINDOW_LENGTH], "sh", -1)
    value_back = shifted(value_sum[:WINDOW_LENGTH], "sh", -1)
    key_total = key_sum[WINDOW_LENGTH:] + key_back
    value_total = value_sum[WINDOW_LENGTH:] + value_back
    query_grad = (query_sum * score_scale).astype(jnp.bfloat16)
    key_grad = (key_total * score_scale).astype(jnp.bfloat16)[:, None]
    value_grad = value_total.astype(jnp.bfloat16)[:, None]

    def back(x):
        x = lax.all_to_all(x, "sl", split_axis=0, concat_axis=1, tiled=True)
        return lax.all_to_all(x, "head", split_axis=0, concat_axis=1, tiled=True)

    return (back(query_grad), back(key_grad), back(value_grad))


def solution(mesh):
    head, seq = mesh.devices.shape
    ring = WINDOW_LENGTH // BLOCK
    grouped = Mesh(mesh.devices.reshape(head, seq // ring, ring), ("head", "sh", "sl"))
    seq_axes = ("sh", "sl")
    placed = (
        P(seq_axes, "head", None),
        P(seq_axes, "head", None),
        P(seq_axes, "head", None),
        P(seq_axes, "head", None),
        P(seq_axes + ("head",), None, None),
        P("head", seq_axes),
        P(seq_axes),
    )
    out = P(seq_axes + ("head",), None, None)
    return jax.shard_map(
        on_device, mesh=grouped, in_specs=placed, out_specs=(out, out, out), check_vma=False
    )
```

profile of v0, /device:TPU:4, one launch (start us, length us, event | category | flops | bytes accessed | tf_op | source)
XLA Modules:
  0.0 181.9 jit_solution(7914831301998009179)
XLA Ops:
  0.6 1.7 copy.58
  2.3 4.5 %all-to-all-start = ((bf16[256,4,128]{2,0,1:T(8,128)(2,1)}), bf16[256,4,128]{2,0,1:T(8,128)(2,1)S(1)}, u32[]{:S(2)}, u32[]{:S(2)}) async-start(bf16[256,4,128]{2,0,1:T(8,128)(2,1)} %copy.58), calls=%async_computation | async-start | bytes 524288 | tf_op jit(solution)/shard_map/all_to_all | solution.py:68
  6.9 10.4 %all-gather = s32[4,1,256]{2,1,0:T(1,128)S(1)} all-gather(s32[1,1,256]{2,1,0:T(1,128)} %bitcast.178), channel_id=1, replica_groups=mesh['head'=4,'sh'=32,'sl'=4] {'sl'}, dimensions={0}, use_global_device_ids=true | all-gather | bytes 5120 | tf_op jit(solution)/shard_map/all_gather | solution.py:72
  17.3 2.1 %copy.61 = bf16[64,32,128]{2,0,1:T(8,128)(2,1)} copy(bf16[64,32,128]{2,1,0:T(8,128)(2,1)} %param.27) | data formatting | bytes 1048576 | tf_op args[4]
  19.4 1.7 copy.60
  21.1 4.0 %all-to-all-start.3 = ((bf16[256,4,128]{2,0,1:T(8,128)(2,1)}), bf16[256,4,128]{2,0,1:T(8,128)(2,1)}, u32[]{:S(2)}, u32[]{:S(2)}) async-start(bf16[256,4,128]{2,0,1:T(8,128)(2,1)} %copy.60), calls=%async_computation.3 | async-start | bytes 524288 | tf_op jit(solution)/shard_map/all_to_all | solution.py:69
  25.2 6.7 %all-to-all-done.3 = bf16[256,4,128]{2,0,1:T(8,128)(2,1)} async-done(((bf16[256,4,128]{2,0,1:T(8,128)(2,1)}), bf16[256,4,128]{2,0,1:T(8,128)(2,1)}, u32[]{:S(2)}, u32[]{:S(2)}) %all-to-all-start.3) | async-done | bytes 262176 | tf_op jit(solution)/shard_map/all_to_all | solution.py:69
  31.8 3.5 %all-to-all-start.4 = ((bf16[64,32,128]{2,0,1:T(8,128)(2,1)}), bf16[64,32,128]{2,0,1:T(8,128)(2,1)S(1)}, u32[]{:S(2)}, u32[]{:S(2)}) async-start(bf16[64,32,128]{2,0,1:T(8,128)(2,1)} %copy.61), calls=%async_computation.4 | async-start | bytes 1048576 | tf_op jit(solution)/shard_map/all_to_all | solution.py:61
  35.3 1.9 %fusion.11 = pred[4,256,1280]{1,2,0:T(8,128)(4,1)S(1)} fusion(s32[4,256]{1,0:T(4,128)S(1)} %bitcast.177, s32[4,1280]{1,0:T(4,128)S(1)} %iota_add_fusion, s32[4,256]{1,0:T(4,128)S(1)} %iota_add_fusion.1), kind=kLoop, calls=%fused_computation.14 | loop fusion | flops 7864320 | bytes 1339392 | tf_op jit(solution)/shard_map/and | solution.py:33
  37.2 3.8 %collective-permute-start = (bf16[1024,128]{1,0:T(8,128)(2,1)S(1)}, bf16[1024,128]{1,0:T(8,128)(2,1)}, u32[]{:S(2)}, u32[]{:S(2)}) collective-permute-start(bf16[1024,128]{1,0:T(8,128)(2,1)S(1)} %bitcast.168), channel_id=1, source_target_pairs={{0,4},{4,8},{8,12},{12,16},{16,20},{20,24},{24,28},{28,32},{32,36}... | collective-permute-start | bytes 786440 | tf_op jit(solution)/shard_map/ppermute | solution.py:15
  41.0 1.1 bitcast_convert_fusion
  42.1 1.9 %copy.59 = bf16[256,8,128]{2,0,1:T(8,128)(2,1)} copy(bf16[256,8,128]{2,1,0:T(8,128)(2,1)} %param.23) | data formatting | bytes 1048576 | tf_op args[0]
  44.7 3.8 %collective-permute-start.1 = (bf16[1024,128]{1,0:T(8,128)(2,1)}, bf16[1024,128]{1,0:T(8,128)(2,1)}, u32[]{:S(2)}, u32[]{:S(2)}) collective-permute-start(bf16[1024,128]{1,0:T(8,128)(2,1)} %bitcast.18), channel_id=1, source_target_pairs={{0,4},{4,8},{8,12},{12,16},{16,20},{20,24},{24,28},{28,32},{32,36}... | collective-permute-start | bytes 786440 | tf_op jit(solution)/shard_map/ppermute | solution.py:15
  48.5 3.2 %all-to-all-start.2 = ((f32[4,2,256]{2,1,0:T(2,128)}), f32[4,2,256]{2,1,0:T(2,128)S(1)}, u32[]{:S(2)}, u32[]{:S(2)}) async-start(f32[4,2,256]{2,1,0:T(2,128)} %all_to_all.161), calls=%async_computation.2 | async-start | bytes 16384 | tf_op jit(solution)/shard_map/all_to_all | solution.py:70
  52.6 1.4 multiply_reduce_fusion
  54.6 2.4 %all-to-all-done.2 = f32[4,2,256]{2,1,0:T(2,128)S(1)} async-done(((f32[4,2,256]{2,1,0:T(2,128)}), f32[4,2,256]{2,1,0:T(2,128)S(1)}, u32[]{:S(2)}, u32[]{:S(2)}) %all-to-all-start.2) | async-done | bytes 8224 | tf_op jit(solution)/shard_map/all_to_all | solution.py:70
  57.0 3.5 %all-to-all-start.1 = ((bf16[256,8,128]{2,0,1:T(8,128)(2,1)}), bf16[256,8,128]{2,0,1:T(8,128)(2,1)S(1)}, u32[]{:S(2)}, u32[]{:S(2)}) async-start(bf16[256,8,128]{2,0,1:T(8,128)(2,1)} %copy.59), calls=%async_computation.1 | async-start | bytes 1048576 | tf_op jit(solution)/shard_map/all_to_all | solution.py:66
  60.5 1.3 fusion.47
  61.8 2.5 %fusion.41 = (bf16[1,1280,128]{2,1,0:T(8,128)(2,1)S(1)}, bf16[1,1280,128]{2,1,0:T(8,128)(2,1)}, bf16[1,1280,128]{2,1,0:T(8,128)(2,1)}, bf16[1,1280,128]{2,1,0:T(8,128)(2,1)}) fusion(bf16[1024,128]{1,0:T(8,128)(2,1)} %collective-permute-done.1, bf16[1024,128]{1,0:T(8,128)(2,1)} %bitcast.18), kind=kLoop, calls=%fused_computation.71 | loop fusion | flops 2621440 | bytes 1835008 | tf_op jit(solution)/shard_map/stack | solution.py:28
  64.4 5.2 %all-to-all-done.1 = bf16[256,8,128]{2,0,1:T(8,128)(2,1)S(1)} async-done(((bf16[256,8,128]{2,0,1:T(8,128)(2,1)}), bf16[256,8,128]{2,0,1:T(8,128)(2,1)S(1)}, u32[]{:S(2)}, u32[]{:S(2)}) %all-to-all-start.1) | async-done | bytes 524320 | tf_op jit(solution)/shard_map/all_to_all | solution.py:66
  69.5 4.1 %all-to-all-start.5 = ((bf16[256,8,128]{2,0,1:T(8,128)(2,1)}), bf16[256,8,128]{2,0,1:T(8,128)(2,1)}, u32[]{:S(2)}, u32[]{:S(2)}) async-start(bf16[256,8,128]{2,0,1:T(8,128)(2,1)} %bitcast.27), calls=%async_computation.5 | async-start | bytes 1048576 | tf_op jit(solution)/shard_map/all_to_all | solution.py:67
  73.7 5.5 %fusion.34 = f32[4,1280,256,2]{2,1,3,0:T(8,128)} fusion(bf16[4,256,2,128]{3,1,2,0:T(8,128)(2,1)S(1)} %bitcast.161, bf16[1,1280,128]{2,1,0:T(8,128)(2,1)S(1)} %get-tuple-element.105, bf16[1,1280,128]{2,1,0:T(8,128)(2,1)S(1)} %get-tuple-element.106, bf16[1,1280,128]{2,1,0:T(8,128)(2,1)S(1)} %get-tuple-element.104, ...), kind=kOutput, calls=%fused_computation.60 | convolution fusion | flops 676331520 | bytes 12320768 | tf_op jit(solution)/shard_map/tigd,tjd->tgij/dot_general | solution.py:35
  79.2 2.6 %all-to-all-done.5 = bf16[256,8,128]{2,0,1:T(8,128)(2,1)} async-done(((bf16[256,8,128]{2,0,1:T(8,128)(2,1)}), bf16[256,8,128]{2,0,1:T(8,128)(2,1)}, u32[]{:S(2)}, u32[]{:S(2)}) %all-to-all-start.5) | async-done | bytes 524320 | tf_op jit(solution)/shard_map/all_to_all | solution.py:67
  81.8 3.2 %all-to-all-start.6 = ((f32[4,2,256]{2,1,0:T(2,128)}), f32[4,2,256]{2,1,0:T(2,128)S(1)}, u32[]{:S(2)}, u32[]{:S(2)}) async-start(f32[4,2,256]{2,1,0:T(2,128)} %all_to_all.173), calls=%async_computation.6 | async-start | bytes 16384 | tf_op jit(solution)/shard_map/all_to_all | solution.py:71
  85.1 5.6 %fusion.13 = f32[4,1280,128]{2,1,0:T(8,128)S(1)} fusion(bf16[4,256,2,128]{3,1,2,0:T(8,128)(2,1)} %bitcast.29, f32[4,1280,256,2]{2,1,3,0:T(8,128)} %fusion.34, f32[4,2,256]{2,1,0:T(2,128)S(1)} %all-to-all-done.2, pred[4,256,1280]{1,2,0:T(8,128)(4,1)S(1)} %fusion.11), kind=kOutput, calls=%fused_computation.16 | convolution fusion | flops 681574400 | bytes 14950400 | tf_op jit(solution)/shard_map/tgij,tigd->tjd/dot_general | solution.py:46
  92.0 7.7 %collective-permute-start.3 = (f32[1024,128]{1,0:T(8,128)}, f32[1024,128]{1,0:T(8,128)}, u32[]{:S(2)}, u32[]{:S(2)}) collective-permute-start(f32[1024,128]{1,0:T(8,128)} %slice.261), channel_id=1, source_target_pairs={{4,0},{8,4},{12,8},{16,12},{20,16},{24,20},{28,24},{32,28},{36,32}... | collective-permute-start | bytes 1572872 | tf_op jit(solution)/shard_map/ppermute | solution.py:15
  99.8 6.2 %fusion.1 = bf16[4,2,256,1280]{2,3,1,0:T(8,128)(2,1)S(1)} fusion(f32[4,1280,256,2]{2,1,3,0:T(8,128)} %fusion.34, bf16[4,256,2,128]{3,1,2,0:T(8,128)(2,1)} %bitcast.29, f32[4,2,256]{2,1,0:T(2,128)S(1)} %all-to-all-done.6, f32[4,2,256]{2,1,0:T(2,128)S(1)} %all-to-all-done.2, pred[4,256,1280]{1,2,0:T(8,128)(4,1)S(1)} %fusion.11, ...), kind=kOutput, calls=%fused_computation.2 | convolution fusion | flops 692060160 | bytes 18890752 | tf_op jit(solution)/shard_map/tigd,tjd->tgij/dot_general | solution.py:39
  106.0 1.5 convolution_bitcast_fusion
  108.9 3.6 %collective-permute-start.2 = (f32[1024,128]{1,0:T(8,128)}, f32[1024,128]{1,0:T(8,128)}, u32[]{:S(2)}, u32[]{:S(2)}) collective-permute-start(f32[1024,128]{1,0:T(8,128)} %slice.253), channel_id=1, source_target_pairs={{4,0},{8,4},{12,8},{16,12},{20,16},{24,20},{28,24},{32,28},{36,32}... | collective-permute-start | bytes 1572872 | tf_op jit(solution)/shard_map/ppermute | solution.py:15
  112.6 1.7 fusion.23
  114.4 1.3 copy.65
  115.7 1.3 copy.66
  117.0 4.8 %all-to-all-start.7 = ((bf16[1024,2,128]{2,1,0:T(2,128)(2,1)}), bf16[1024,2,128]{2,1,0:T(2,128)(2,1)S(1)}, u32[]{:S(2)}, u32[]{:S(2)}) async-start(bf16[1024,2,128]{2,1,0:T(2,128)(2,1)} %copy.66), calls=%async_computation.7 | async-start | bytes 1048576 | tf_op jit(solution)/shard_map/all_to_all | solution.py:93
  121.8 1.1 fusion.53
  125.0 4.9 %all-to-all-done.7 = bf16[1024,2,128]{2,1,0:T(2,128)(2,1)S(1)} async-done(((bf16[1024,2,128]{2,1,0:T(2,128)(2,1)}), bf16[1024,2,128]{2,1,0:T(2,128)(2,1)S(1)}, u32[]{:S(2)}, u32[]{:S(2)}) %all-to-all-start.7) | async-done | bytes 524320 | tf_op jit(solution)/shard_map/all_to_all | solution.py:93
  129.8 3.4 %all-to-all-start.11 = ((bf16[4,2,16384]{2,1,0:T(2,128)(2,1)}), bf16[4,2,16384]{2,1,0:T(2,128)(2,1)S(1)}, u32[]{:S(2)}, u32[]{:S(2)}) async-start(bf16[4,2,16384]{2,1,0:T(2,128)(2,1)} %reshape.299), calls=%async_computation.11 | async-start | bytes 524288 | tf_op jit(solution)/shard_map/all_to_all | solution.py:93
  133.3 1.1 fusion.52
  136.0 3.9 %all-to-all-done.11 = bf16[4,2,16384]{2,1,0:T(2,128)(2,1)S(1)} async-done(((bf16[4,2,16384]{2,1,0:T(2,128)(2,1)}), bf16[4,2,16384]{2,1,0:T(2,128)(2,1)S(1)}, u32[]{:S(2)}, u32[]{:S(2)}) %all-to-all-start.11) | async-done | bytes 262176 | tf_op jit(solution)/shard_map/all_to_all | solution.py:93
  139.9 3.4 %all-to-all-start.9 = ((bf16[4,2,16384]{2,1,0:T(2,128)(2,1)}), bf16[4,2,16384]{2,1,0:T(2,128)(2,1)S(1)}, u32[]{:S(2)}, u32[]{:S(2)}) async-start(bf16[4,2,16384]{2,1,0:T(2,128)(2,1)} %reshape.297), calls=%async_computation.9 | async-start | bytes 524288 | tf_op jit(solution)/shard_map/all_to_all | solution.py:93
  143.4 1.1 copy.69
  144.6 5.4 %all-to-all-done.9 = bf16[4,2,16384]{2,1,0:T(2,128)(2,1)S(1)} async-done(((bf16[4,2,16384]{2,1,0:T(2,128)(2,1)}), bf16[4,2,16384]{2,1,0:T(2,128)(2,1)S(1)}, u32[]{:S(2)}, u32[]{:S(2)}) %all-to-all-start.9) | async-done | bytes 262176 | tf_op jit(solution)/shard_map/all_to_all | solution.py:93
  150.0 3.5 %all-to-all-start.8 = ((bf16[256,8,128]{2,1,0:T(8,128)(2,1)}), bf16[256,8,128]{2,1,0:T(8,128)(2,1)S(1)}, u32[]{:S(2)}, u32[]{:S(2)}) async-start(bf16[256,8,128]{2,1,0:T(8,128)(2,1)} %copy.69), calls=%async_computation.8 | async-start | bytes 1048576 | tf_op jit(solution)/shard_map/all_to_all | solution.py:94
  153.8 0.9 copy.75
  154.7 7.6 %all-to-all-done.8 = bf16[256,8,128]{2,1,0:T(8,128)(2,1)S(1)} async-done(((bf16[256,8,128]{2,1,0:T(8,128)(2,1)}), bf16[256,8,128]{2,1,0:T(8,128)(2,1)S(1)}, u32[]{:S(2)}, u32[]{:S(2)}) %all-to-all-start.8) | async-done | bytes 524320 | tf_op jit(solution)/shard_map/all_to_all | solution.py:94
  162.3 3.4 %all-to-all-start.12 = ((bf16[256,4,128]{2,1,0:T(4,128)(2,1)}), bf16[256,4,128]{2,1,0:T(4,128)(2,1)S(1)}, u32[]{:S(2)}, u32[]{:S(2)}) async-start(bf16[256,4,128]{2,1,0:T(4,128)(2,1)} %copy.75), calls=%async_computation.12 | async-start | bytes 524288 | tf_op jit(solution)/shard_map/all_to_all | solution.py:94
  166.9 4.7 %all-to-all-done.12 = bf16[256,4,128]{2,1,0:T(4,128)(2,1)S(1)} async-done(((bf16[256,4,128]{2,1,0:T(4,128)(2,1)}), bf16[256,4,128]{2,1,0:T(4,128)(2,1)S(1)}, u32[]{:S(2)}, u32[]{:S(2)}) %all-to-all-start.12) | async-done | bytes 262176 | tf_op jit(solution)/shard_map/all_to_all | solution.py:94
  171.7 3.4 %all-to-all-start.10 = ((bf16[256,4,128]{2,1,0:T(4,128)(2,1)}), bf16[256,4,128]{2,1,0:T(4,128)(2,1)S(1)}, u32[]{:S(2)}, u32[]{:S(2)}) async-start(bf16[256,4,128]{2,1,0:T(4,128)(2,1)} %copy.72), calls=%async_computation.10 | async-start | bytes 524288 | tf_op jit(solution)/shard_map/all_to_all | solution.py:94
  176.8 4.3 %all-to-all-done.10 = bf16[256,4,128]{2,1,0:T(4,128)(2,1)S(1)} async-done(((bf16[256,4,128]{2,1,0:T(4,128)(2,1)}), bf16[256,4,128]{2,1,0:T(4,128)(2,1)S(1)}, u32[]{:S(2)}, u32[]{:S(2)}) %all-to-all-start.10) | async-done | bytes 262176 | tf_op jit(solution)/shard_map/all_to_all | solution.py:94
  (57 shorter events, 12.8 us)
Async XLA Ops:
  2.3 18.7 %all-to-all-start = ((bf16[256,4,128]{2,0,1:T(8,128)(2,1)}), bf16[256,4,128]{2,0,1:T(8,128)(2,1)S(1)}, u32[]{:S(2)}, u32[]{:S(2)}) async-start(bf16[256,4,128]{2,0,1:T(8,128)(2,1)} %copy.58), calls=%async_computation | async-start | bytes 524288 | tf_op jit(solution)/shard_map/all_to_all | solution.py:68
  21.1 23.0 %copy-start.4 = (bf16[256,4,128]{2,0,1:T(8,128)(2,1)}, bf16[256,4,128]{2,0,1:T(8,128)(2,1)S(1)}, u32[]{:S(2)}) copy-start(bf16[256,4,128]{2,0,1:T(8,128)(2,1)S(1)} %all-to-all-done) | copy-start | bytes 786436
  21.1 10.8 %all-to-all-start.3 = ((bf16[256,4,128]{2,0,1:T(8,128)(2,1)}), bf16[256,4,128]{2,0,1:T(8,128)(2,1)}, u32[]{:S(2)}, u32[]{:S(2)}) async-start(bf16[256,4,128]{2,0,1:T(8,128)(2,1)} %copy.60), calls=%async_computation.3 | async-start | bytes 524288 | tf_op jit(solution)/shard_map/all_to_all | solution.py:69
  25.1 18.9 %copy-start.6 = (f32[8,256]{1,0:T(8,128)S(1)}, f32[8,256]{1,0:T(8,128)}, u32[]{:S(2)}) copy-start(f32[8,256]{1,0:T(8,128)} %param.28) | copy-start | bytes 24580
  31.8 16.6 %all-to-all-start.4 = ((bf16[64,32,128]{2,0,1:T(8,128)(2,1)}), bf16[64,32,128]{2,0,1:T(8,128)(2,1)S(1)}, u32[]{:S(2)}, u32[]{:S(2)}) async-start(bf16[64,32,128]{2,0,1:T(8,128)(2,1)} %copy.61), calls=%async_computation.4 | async-start | bytes 1048576 | tf_op jit(solution)/shard_map/all_to_all | solution.py:61
  37.2 23.3 %collective-permute-start = (bf16[1024,128]{1,0:T(8,128)(2,1)S(1)}, bf16[1024,128]{1,0:T(8,128)(2,1)}, u32[]{:S(2)}, u32[]{:S(2)}) collective-permute-start(bf16[1024,128]{1,0:T(8,128)(2,1)S(1)} %bitcast.168), channel_id=1, source_target_pairs={{0,4},{4,8},{8,12},{12,16},{16,20},{20,24},{24,28},{28,32},{32,36}... | collective-permute-start | bytes 786440 | tf_op jit(solution)/shard_map/ppermute | solution.py:15
  44.7 17.2 %collective-permute-start.1 = (bf16[1024,128]{1,0:T(8,128)(2,1)}, bf16[1024,128]{1,0:T(8,128)(2,1)}, u32[]{:S(2)}, u32[]{:S(2)}) collective-permute-start(bf16[1024,128]{1,0:T(8,128)(2,1)} %bitcast.18), channel_id=1, source_target_pairs={{0,4},{4,8},{8,12},{12,16},{16,20},{20,24},{24,28},{28,32},{32,36}... | collective-permute-start | bytes 786440 | tf_op jit(solution)/shard_map/ppermute | solution.py:15
  48.5 8.5 %all-to-all-start.2 = ((f32[4,2,256]{2,1,0:T(2,128)}), f32[4,2,256]{2,1,0:T(2,128)S(1)}, u32[]{:S(2)}, u32[]{:S(2)}) async-start(f32[4,2,256]{2,1,0:T(2,128)} %all_to_all.161), calls=%async_computation.2 | async-start | bytes 16384 | tf_op jit(solution)/shard_map/all_to_all | solution.py:70
  52.6 7.9 %copy-start.5 = (bf16[256,4,128]{2,0,1:T(8,128)(2,1)S(1)}, bf16[256,4,128]{2,0,1:T(8,128)(2,1)}, u32[]{:S(2)}) copy-start(bf16[256,4,128]{2,0,1:T(8,128)(2,1)} %copy-done.4) | copy-start | bytes 786436
  57.0 12.5 %all-to-all-start.1 = ((bf16[256,8,128]{2,0,1:T(8,128)(2,1)}), bf16[256,8,128]{2,0,1:T(8,128)(2,1)S(1)}, u32[]{:S(2)}, u32[]{:S(2)}) async-start(bf16[256,8,128]{2,0,1:T(8,128)(2,1)} %copy.59), calls=%async_computation.1 | async-start | bytes 1048576 | tf_op jit(solution)/shard_map/all_to_all | solution.py:66
  61.8 17.4 %copy-start = (bf16[1,1280,128]{2,1,0:T(8,128)(2,1)}, bf16[1,1280,128]{2,1,0:T(8,128)(2,1)S(1)}, u32[]{:S(2)}) copy-start(bf16[1,1280,128]{2,1,0:T(8,128)(2,1)S(1)} %get-tuple-element.105) | copy-start | bytes 983044
  61.8 17.4 %copy-start.2 = (bf16[1,1280,128]{2,1,0:T(8,128)(2,1)}, bf16[1,1280,128]{2,1,0:T(8,128)(2,1)S(1)}, u32[]{:S(2)}) copy-start(bf16[1,1280,128]{2,1,0:T(8,128)(2,1)S(1)} %get-tuple-element.106) | copy-start | bytes 983044
  69.5 12.3 %all-to-all-start.5 = ((bf16[256,8,128]{2,0,1:T(8,128)(2,1)}), bf16[256,8,128]{2,0,1:T(8,128)(2,1)}, u32[]{:S(2)}, u32[]{:S(2)}) async-start(bf16[256,8,128]{2,0,1:T(8,128)(2,1)} %bitcast.27), calls=%async_computation.5 | async-start | bytes 1048576 | tf_op jit(solution)/shard_map/all_to_all | solution.py:67
  81.8 17.9 %all-to-all-start.6 = ((f32[4,2,256]{2,1,0:T(2,128)}), f32[4,2,256]{2,1,0:T(2,128)S(1)}, u32[]{:S(2)}, u32[]{:S(2)}) async-start(f32[4,2,256]{2,1,0:T(2,128)} %all_to_all.173), calls=%async_computation.6 | async-start | bytes 16384 | tf_op jit(solution)/shard_map/all_to_all | solution.py:71
  92.0 29.7 %collective-permute-start.3 = (f32[1024,128]{1,0:T(8,128)}, f32[1024,128]{1,0:T(8,128)}, u32[]{:S(2)}, u32[]{:S(2)}) collective-permute-start(f32[1024,128]{1,0:T(8,128)} %slice.261), channel_id=1, source_target_pairs={{4,0},{8,4},{12,8},{16,12},{20,16},{24,20},{28,24},{32,28},{36,32}... | collective-permute-start | bytes 1572872 | tf_op jit(solution)/shard_map/ppermute | solution.py:15
  107.9 4.7 %copy-start.1 = (bf16[1,1280,128]{2,1,0:T(8,128)(2,1)S(1)}, bf16[1,1280,128]{2,1,0:T(8,128)(2,1)}, u32[]{:S(2)}) copy-start(bf16[1,1280,128]{2,1,0:T(8,128)(2,1)} %copy-done) | copy-start | bytes 983044
  107.9 4.7 %copy-start.3 = (bf16[1,1280,128]{2,1,0:T(8,128)(2,1)S(1)}, bf16[1,1280,128]{2,1,0:T(8,128)(2,1)}, u32[]{:S(2)}) copy-start(bf16[1,1280,128]{2,1,0:T(8,128)(2,1)} %copy-done.2) | copy-start | bytes 983044
  108.9 24.3 %collective-permute-start.2 = (f32[1024,128]{1,0:T(8,128)}, f32[1024,128]{1,0:T(8,128)}, u32[]{:S(2)}, u32[]{:S(2)}) collective-permute-start(f32[1024,128]{1,0:T(8,128)} %slice.253), channel_id=1, source_target_pairs={{4,0},{8,4},{12,8},{16,12},{20,16},{24,20},{28,24},{32,28},{36,32}... | collective-permute-start | bytes 1572872 | tf_op jit(solution)/shard_map/ppermute | solution.py:15
  117.0 12.8 %all-to-all-start.7 = ((bf16[1024,2,128]{2,1,0:T(2,128)(2,1)}), bf16[1024,2,128]{2,1,0:T(2,128)(2,1)S(1)}, u32[]{:S(2)}, u32[]{:S(2)}) async-start(bf16[1024,2,128]{2,1,0:T(2,128)(2,1)} %copy.66), calls=%async_computation.7 | async-start | bytes 1048576 | tf_op jit(solution)/shard_map/all_to_all | solution.py:93
  129.8 10.1 %all-to-all-start.11 = ((bf16[4,2,16384]{2,1,0:T(2,128)(2,1)}), bf16[4,2,16384]{2,1,0:T(2,128)(2,1)S(1)}, u32[]{:S(2)}, u32[]{:S(2)}) async-start(bf16[4,2,16384]{2,1,0:T(2,128)(2,1)} %reshape.299), calls=%async_computation.11 | async-start | bytes 524288 | tf_op jit(solution)/shard_map/all_to_all | solution.py:93
  139.9 10.1 %all-to-all-start.9 = ((bf16[4,2,16384]{2,1,0:T(2,128)(2,1)}), bf16[4,2,16384]{2,1,0:T(2,128)(2,1)S(1)}, u32[]{:S(2)}, u32[]{:S(2)}) async-start(bf16[4,2,16384]{2,1,0:T(2,128)(2,1)} %reshape.297), calls=%async_computation.9 | async-start | bytes 524288 | tf_op jit(solution)/shard_map/all_to_all | solution.py:93
  150.0 12.3 %all-to-all-start.8 = ((bf16[256,8,128]{2,1,0:T(8,128)(2,1)}), bf16[256,8,128]{2,1,0:T(8,128)(2,1)S(1)}, u32[]{:S(2)}, u32[]{:S(2)}) async-start(bf16[256,8,128]{2,1,0:T(8,128)(2,1)} %copy.69), calls=%async_computation.8 | async-start | bytes 1048576 | tf_op jit(solution)/shard_map/all_to_all | solution.py:94
  162.3 9.4 %all-to-all-start.12 = ((bf16[256,4,128]{2,1,0:T(4,128)(2,1)}), bf16[256,4,128]{2,1,0:T(4,128)(2,1)S(1)}, u32[]{:S(2)}, u32[]{:S(2)}) async-start(bf16[256,4,128]{2,1,0:T(4,128)(2,1)} %copy.75), calls=%async_computation.12 | async-start | bytes 524288 | tf_op jit(solution)/shard_map/all_to_all | solution.py:94
  171.7 9.4 %all-to-all-start.10 = ((bf16[256,4,128]{2,1,0:T(4,128)(2,1)}), bf16[256,4,128]{2,1,0:T(4,128)(2,1)S(1)}, u32[]{:S(2)}, u32[]{:S(2)}) async-start(bf16[256,4,128]{2,1,0:T(4,128)(2,1)} %copy.72), calls=%async_computation.10 | async-start | bytes 524288 | tf_op jit(solution)/shard_map/all_to_all | solution.py:94
where the time goes:
time: 183 us; the launch traced here: 182 us
  starting transfers between devices  66.9 us (37%)
  waiting for transfers between devices  47.6 us (26%)
  local copies, waits for them, and re-layouts  22.3 us (12%)
  matrix products  20.6 us (11%)
  other arithmetic  12.9 us (7%)
  blocking collectives  10.4 us (6%)
    ppermute x4, starting transfers between devices, shifted(): return lax.ppermute(value, axis, pairs)  19 us
    all_to_all x3, waiting for transfers between devices, back(): return lax.all_to_all(x, 'head', split_axis=0, concat_axis=1, tiled=True)  16.6 us
    all_to_all x3, waiting for transfers between devices, back(): x = lax.all_to_all(x, 'sl', split_axis=0, concat_axis=1, tiled=True)  14.2 us
    all_to_all x3, starting transfers between devices, back(): x = lax.all_to_all(x, 'sl', split_axis=0, concat_axis=1, tiled=True)  11.6 us
    all_gather x1, blocking collectives, on_device(): start_g = lax.all_gather(pair_start, 'sl', axis=0, tiled=True)  10.4 us
    all_to_all x3, starting transfers between devices, back(): return lax.all_to_all(x, 'head', split_axis=0, concat_axis=1, tiled=True)  10.3 us
    unnamed x25, local copies, waits for them, and re-layouts  9.52 us
    all_to_all x1, waiting for transfers between devices, on_device(): lax.all_to_all(value_matrix, 'sl', split_axis=1, concat_axis=0, tiled=True)  6.65 us
  transfers between devices with their start and end apart: 17, of which 10 were waited for; matrix products, arithmetic and copies ran while one was open for 29% of the time, Pallas kernels for 0%

commit v1 on v0

--- a/solution.py
+++ b/solution.py
@@ -66,7 +66,20 @@
     query_g = lax.all_to_all(queries, "sl", split_axis=1, concat_axis=0, tiled=True)
     grad_g = lax.all_to_all(grad_rows, "sl", split_axis=1, concat_axis=0, tiled=True)
     key_g = lax.all_to_all(normed_keys, "sl", split_axis=1, concat_axis=0, tiled=True)
-    value_g = lax.all_to_all(value_matrix, "sl", split_axis=1, concat_axis=0, tiled=True)
+
+    def bring_yards(pos_dim, in_dim, point):
+        view_out = jnp.concatenate(
+            lax.all_to_all(
+                jnp.stack(jnp.split(point, lax.axis_size("sl"), axis=in_dim)),
+                concat_axis=0,
+                split_axis=0,
+                axis_name="sl",
+            ),
+            axis=pos_dim,
+        )
+        return view_out
+
+    value_g = bring_yards(0, 1, point=value_matrix)
     logsum_g = lax.all_to_all(row_log_total, "sl", split_axis=0, concat_axis=1, tiled=True)
     delta_g = lax.all_to_all(delta_rows, "sl", split_axis=0, concat_axis=1, tiled=True)
     start_g = lax.all_gather(pair_start, "sl", axis=0, tiled=True)

time: 183 us -> 183 us (level)
    unnamed x25 -> x28, local copies, waits for them, and re-layouts: 9.52 us -> 6.85 us
    split x0 -> x1, local copies, waits for them, and re-layouts: none -> 2.03 us  [bring_yards(): jnp.split(point, lax.axis_size('sl'), axis=in_dim)]
where the time goes in v1:
time: 183 us; the launch traced here: 182 us
  starting transfers between devices  67.1 us (37%)
  waiting for transfers between devices  47.7 us (26%)
  local copies, waits for them, and re-layouts  21.7 us (12%)
  matrix products  20.6 us (11%)
  other arithmetic  13.6 us (7%)
  blocking collectives  10.2 us (6%)
    ppermute x4, starting transfers between devices, shifted(): return lax.ppermute(value, axis, pairs)  19.1 us
    all_to_all x3, waiting for transfers between devices, back(): return lax.all_to_all(x, 'head', split_axis=0, concat_axis=1, tiled=True)  16.6 us
    all_to_all x3, waiting for transfers between devices, back(): x = lax.all_to_all(x, 'sl', split_axis=0, concat_axis=1, tiled=True)  14.2 us
    all_to_all x3, starting transfers between devices, back(): x = lax.all_to_all(x, 'sl', split_axis=0, concat_axis=1, tiled=True)  11.5 us
    all_to_all x3, starting transfers between devices, back(): return lax.all_to_all(x, 'head', split_axis=0, concat_axis=1, tiled=True)  10.3 us
    all_gather x1, blocking collectives, on_device(): start_g = lax.all_gather(pair_start, 'sl', axis=0, tiled=True)  10.2 us
    unnamed x28, local copies, waits for them, and re-layouts  6.85 us
    all_to_all x1, waiting for transfers between devices, bring_yards(): lax.all_to_all(jnp.stack(jnp.split(point, lax.axis_size('sl'), axis=in_di...  6.65 us
  transfers between devices with their start and end apart: 17, of which 10 were waited for; matrix products, arithmetic and copies ran while one was open for 29% of the time, Pallas kernels for 0%

profile of v1, /device:TPU:4, one launch (start us, length us, event | category | flops | bytes accessed | tf_op | source)
XLA Modules:
  0.0 182.0 jit_solution(3846939707460195515)
XLA Ops:
  0.7 1.7 copy.69
  2.4 4.5 %all-to-all-start = ((bf16[256,4,128]{2,0,1:T(8,128)(2,1)}), bf16[256,4,128]{2,0,1:T(8,128)(2,1)S(1)}, u32[]{:S(2)}, u32[]{:S(2)}) async-start(bf16[256,4,128]{2,0,1:T(8,128)(2,1)} %copy.69), calls=%async_computation | async-start | bytes 524288 | tf_op jit(solution)/shard_map/all_to_all | solution.py:68
  6.9 2.0 %fusion.59 = (bf16[256,1,128]{2,1,0:T(2,128)(2,1)S(1)}, bf16[256,1,128]{2,1,0:T(2,128)(2,1)S(1)}, bf16[256,1,128]{2,1,0:T(2,128)(2,1)S(1)}, bf16[256,1,128]{2,1,0:T(2,128)(2,1)S(1)}) fusion(bf16[256,4,128]{2,1,0:T(4,128)(2,1)} %param.25), kind=kLoop, calls=%fused_computation.103 | loop fusion | bytes 524288 | tf_op jit(solution)/shard_map/split | solution.py:73
  9.0 10.2 %all-gather = s32[4,1,256]{2,1,0:T(1,128)S(1)} all-gather(s32[1,1,256]{2,1,0:T(1,128)S(1)} %bitcast.182), channel_id=1, replica_groups=mesh['head'=4,'sh'=32,'sl'=4] {'sl'}, dimensions={0}, use_global_device_ids=true | all-gather | bytes 5120 | tf_op jit(solution)/shard_map/all_gather | solution.py:85
  19.3 1.0 copy.75
  21.0 4.1 %all-to-all-start.3 = ((bf16[4,256,1,128]{3,1,2,0:T(8,128)(2,1)}), bf16[4,256,1,128]{3,1,2,0:T(8,128)(2,1)}, u32[]{:S(2)}, u32[]{:S(2)}) async-start(bf16[4,256,1,128]{3,1,2,0:T(8,128)(2,1)} %pad_maximum_fusion.2), calls=%async_computation.3 | async-start | bytes 524288 | tf_op jit(solution)/shard_map/all_to_all | solution.py:72
  25.1 6.7 %all-to-all-done.3 = bf16[4,256,1,128]{3,1,2,0:T(8,128)(2,1)} async-done(((bf16[4,256,1,128]{3,1,2,0:T(8,128)(2,1)}), bf16[4,256,1,128]{3,1,2,0:T(8,128)(2,1)}, u32[]{:S(2)}, u32[]{:S(2)}) %all-to-all-start.3) | async-done | bytes 262176 | tf_op jit(solution)/shard_map/all_to_all | solution.py:72
  31.8 3.5 %all-to-all-start.4 = ((bf16[64,32,128]{2,0,1:T(8,128)(2,1)}), bf16[64,32,128]{2,0,1:T(8,128)(2,1)S(1)}, u32[]{:S(2)}, u32[]{:S(2)}) async-start(bf16[64,32,128]{2,0,1:T(8,128)(2,1)} %copy.75), calls=%async_computation.4 | async-start | bytes 1048576 | tf_op jit(solution)/shard_map/all_to_all | solution.py:61
  35.3 1.9 %fusion.11 = pred[4,256,1280]{1,2,0:T(8,128)(4,1)S(1)} fusion(s32[4,256]{1,0:T(4,128)S(1)} %bitcast.181, s32[4,1280]{1,0:T(4,128)S(1)} %iota_add_fusion, s32[4,256]{1,0:T(4,128)S(1)} %iota_add_fusion.1), kind=kLoop, calls=%fused_computation.14 | loop fusion | flops 7864320 | bytes 1339392 | tf_op jit(solution)/shard_map/and | solution.py:33
  37.1 3.8 %collective-permute-start = (bf16[1024,128]{1,0:T(8,128)(2,1)S(1)}, bf16[1024,128]{1,0:T(8,128)(2,1)}, u32[]{:S(2)}, u32[]{:S(2)}) collective-permute-start(bf16[1024,128]{1,0:T(8,128)(2,1)S(1)} %bitcast.172), channel_id=1, source_target_pairs={{0,4},{4,8},{8,12},{12,16},{16,20},{20,24},{24,28},{28,32},{32,36}... | collective-permute-start | bytes 786440 | tf_op jit(solution)/shard_map/ppermute | solution.py:15
  41.0 1.1 bitcast_convert_fusion
  42.1 1.9 %copy.70 = bf16[256,8,128]{2,0,1:T(8,128)(2,1)} copy(bf16[256,8,128]{2,1,0:T(8,128)(2,1)} %param.23) | data formatting | bytes 1048576 | tf_op args[0]
  44.6 3.8 %collective-permute-start.1 = (bf16[1024,128]{1,0:T(8,128)(2,1)}, bf16[1024,128]{1,0:T(8,128)(2,1)}, u32[]{:S(2)}, u32[]{:S(2)}) collective-permute-start(bf16[1024,128]{1,0:T(8,128)(2,1)} %bitcast.20), channel_id=1, source_target_pairs={{0,4},{4,8},{8,12},{12,16},{16,20},{20,24},{24,28},{28,32},{32,36}... | collective-permute-start | bytes 786440 | tf_op jit(solution)/shard_map/ppermute | solution.py:15
  48.4 3.2 %all-to-all-start.2 = ((f32[4,2,256]{2,1,0:T(2,128)}), f32[4,2,256]{2,1,0:T(2,128)S(1)}, u32[]{:S(2)}, u32[]{:S(2)}) async-start(f32[4,2,256]{2,1,0:T(2,128)} %all_to_all.153), calls=%async_computation.2 | async-start | bytes 16384 | tf_op jit(solution)/shard_map/all_to_all | solution.py:83
  52.6 1.4 multiply_reduce_fusion
  54.6 2.4 %all-to-all-done.2 = f32[4,2,256]{2,1,0:T(2,128)S(1)} async-done(((f32[4,2,256]{2,1,0:T(2,128)}), f32[4,2,256]{2,1,0:T(2,128)S(1)}, u32[]{:S(2)}, u32[]{:S(2)}) %all-to-all-start.2) | async-done | bytes 8224 | tf_op jit(solution)/shard_map/all_to_all | solution.py:83
  57.0 3.5 %all-to-all-start.1 = ((bf16[256,8,128]{2,0,1:T(8,128)(2,1)}), bf16[256,8,128]{2,0,1:T(8,128)(2,1)S(1)}, u32[]{:S(2)}, u32[]{:S(2)}) async-start(bf16[256,8,128]{2,0,1:T(8,128)(2,1)} %copy.70), calls=%async_computation.1 | async-start | bytes 1048576 | tf_op jit(solution)/shard_map/all_to_all | solution.py:66
  60.5 1.3 fusion.47
  61.8 2.5 %fusion.41 = (bf16[1,1280,128]{2,1,0:T(8,128)(2,1)S(1)}, bf16[1,1280,128]{2,1,0:T(8,128)(2,1)}, bf16[1,1280,128]{2,1,0:T(8,128)(2,1)}, bf16[1,1280,128]{2,1,0:T(8,128)(2,1)}) fusion(bf16[1024,128]{1,0:T(8,128)(2,1)} %collective-permute-done.1, bf16[1024,128]{1,0:T(8,128)(2,1)} %bitcast.20), kind=kLoop, calls=%fused_computation.71 | loop fusion | flops 2621440 | bytes 1835008 | tf_op jit(solution)/shard_map/stack | solution.py:28
  64.3 5.2 %all-to-all-done.1 = bf16[256,8,128]{2,0,1:T(8,128)(2,1)S(1)} async-done(((bf16[256,8,128]{2,0,1:T(8,128)(2,1)}), bf16[256,8,128]{2,0,1:T(8,128)(2,1)S(1)}, u32[]{:S(2)}, u32[]{:S(2)}) %all-to-all-start.1) | async-done | bytes 524320 | tf_op jit(solution)/shard_map/all_to_all | solution.py:66
  69.5 4.1 %all-to-all-start.5 = ((bf16[256,8,128]{2,0,1:T(8,128)(2,1)}), bf16[256,8,128]{2,0,1:T(8,128)(2,1)}, u32[]{:S(2)}, u32[]{:S(2)}) async-start(bf16[256,8,128]{2,0,1:T(8,128)(2,1)} %bitcast.29), calls=%async_computation.5 | async-start | bytes 1048576 | tf_op jit(solution)/shard_map/all_to_all | solution.py:67
  73.6 5.6 %fusion.34 = f32[4,1280,256,2]{2,1,3,0:T(8,128)} fusion(bf16[4,256,2,128]{3,1,2,0:T(8,128)(2,1)S(1)} %bitcast.165, bf16[1,1280,128]{2,1,0:T(8,128)(2,1)S(1)} %get-tuple-element.105, bf16[1,1280,128]{2,1,0:T(8,128)(2,1)S(1)} %get-tuple-element.106, bf16[1,1280,128]{2,1,0:T(8,128)(2,1)S(1)} %get-tuple-element.104, ...), kind=kOutput, calls=%fused_computation.60 | convolution fusion | flops 676331520 | bytes 12320768 | tf_op jit(solution)/shard_map/tigd,tjd->tgij/dot_general | solution.py:35
  79.2 2.6 %all-to-all-done.5 = bf16[256,8,128]{2,0,1:T(8,128)(2,1)} async-done(((bf16[256,8,128]{2,0,1:T(8,128)(2,1)}), bf16[256,8,128]{2,0,1:T(8,128)(2,1)}, u32[]{:S(2)}, u32[]{:S(2)}) %all-to-all-start.5) | async-done | bytes 524320 | tf_op jit(solution)/shard_map/all_to_all | solution.py:67
  81.8 3.2 %all-to-all-start.6 = ((f32[4,2,256]{2,1,0:T(2,128)}), f32[4,2,256]{2,1,0:T(2,128)S(1)}, u32[]{:S(2)}, u32[]{:S(2)}) async-start(f32[4,2,256]{2,1,0:T(2,128)} %all_to_all.163), calls=%async_computation.6 | async-start | bytes 16384 | tf_op jit(solution)/shard_map/all_to_all | solution.py:84
  85.0 5.6 %fusion.13 = f32[4,1280,128]{2,1,0:T(8,128)S(1)} fusion(bf16[4,256,2,128]{3,1,2,0:T(8,128)(2,1)} %bitcast.31, f32[4,1280,256,2]{2,1,3,0:T(8,128)} %fusion.34, f32[4,2,256]{2,1,0:T(2,128)S(1)} %all-to-all-done.2, pred[4,256,1280]{1,2,0:T(8,128)(4,1)S(1)} %fusion.11), kind=kOutput, calls=%fused_computation.16 | convolution fusion | flops 681574400 | bytes 14950400 | tf_op jit(solution)/shard_map/tgij,tigd->tjd/dot_general | solution.py:46
  92.0 7.7 %collective-permute-start.3 = (f32[1024,128]{1,0:T(8,128)}, f32[1024,128]{1,0:T(8,128)}, u32[]{:S(2)}, u32[]{:S(2)}) collective-permute-start(f32[1024,128]{1,0:T(8,128)} %slice.261), channel_id=1, source_target_pairs={{4,0},{8,4},{12,8},{16,12},{20,16},{24,20},{28,24},{32,28},{36,32}... | collective-permute-start | bytes 1572872 | tf_op jit(solution)/shard_map/ppermute | solution.py:15
  99.7 6.2 %fusion.1 = bf16[4,2,256,1280]{2,3,1,0:T(8,128)(2,1)S(1)} fusion(f32[4,1280,256,2]{2,1,3,0:T(8,128)} %fusion.34, bf16[4,256,2,128]{3,1,2,0:T(8,128)(2,1)} %bitcast.31, f32[4,2,256]{2,1,0:T(2,128)S(1)} %all-to-all-done.6, f32[4,2,256]{2,1,0:T(2,128)S(1)} %all-to-all-done.2, pred[4,256,1280]{1,2,0:T(8,128)(4,1)S(1)} %fusion.11, ...), kind=kOutput, calls=%fused_computation.2 | convolution fusion | flops 692060160 | bytes 18890752 | tf_op jit(solution)/shard_map/tigd,tjd->tgij/dot_general | solution.py:39
  105.9 1.5 convolution_bitcast_fusion
  108.9 3.8 %collective-permute-start.2 = (f32[1024,128]{1,0:T(8,128)}, f32[1024,128]{1,0:T(8,128)}, u32[]{:S(2)}, u32[]{:S(2)}) collective-permute-start(f32[1024,128]{1,0:T(8,128)} %slice.253), channel_id=1, source_target_pairs={{4,0},{8,4},{12,8},{16,12},{20,16},{24,20},{28,24},{32,28},{36,32}... | collective-permute-start | bytes 1572872 | tf_op jit(solution)/shard_map/ppermute | solution.py:15
  112.7 1.8 fusion.23
  114.5 1.3 copy.79
  115.8 1.3 copy.80
  117.2 4.7 %all-to-all-start.7 = ((bf16[1024,2,128]{2,1,0:T(2,128)(2,1)}), bf16[1024,2,128]{2,1,0:T(2,128)(2,1)S(1)}, u32[]{:S(2)}, u32[]{:S(2)}) async-start(bf16[1024,2,128]{2,1,0:T(2,128)(2,1)} %copy.80), calls=%async_computation.7 | async-start | bytes 1048576 | tf_op jit(solution)/shard_map/all_to_all | solution.py:106
  121.9 1.1 fusion.53
  125.1 4.9 %all-to-all-done.7 = bf16[1024,2,128]{2,1,0:T(2,128)(2,1)S(1)} async-done(((bf16[1024,2,128]{2,1,0:T(2,128)(2,1)}), bf16[1024,2,128]{2,1,0:T(2,128)(2,1)S(1)}, u32[]{:S(2)}, u32[]{:S(2)}) %all-to-all-start.7) | async-done | bytes 524320 | tf_op jit(solution)/shard_map/all_to_all | solution.py:106
  130.0 3.4 %all-to-all-start.11 = ((bf16[4,2,16384]{2,1,0:T(2,128)(2,1)}), bf16[4,2,16384]{2,1,0:T(2,128)(2,1)S(1)}, u32[]{:S(2)}, u32[]{:S(2)}) async-start(bf16[4,2,16384]{2,1,0:T(2,128)(2,1)} %reshape.298), calls=%async_computation.11 | async-start | bytes 524288 | tf_op jit(solution)/shard_map/all_to_all | solution.py:106
  133.4 1.1 fusion.52
  136.1 3.9 %all-to-all-done.11 = bf16[4,2,16384]{2,1,0:T(2,128)(2,1)S(1)} async-done(((bf16[4,2,16384]{2,1,0:T(2,128)(2,1)}), bf16[4,2,16384]{2,1,0:T(2,128)(2,1)S(1)}, u32[]{:S(2)}, u32[]{:S(2)}) %all-to-all-start.11) | async-done | bytes 262176 | tf_op jit(solution)/shard_map/all_to_all | solution.py:106
  140.0 3.4 %all-to-all-start.9 = ((bf16[4,2,16384]{2,1,0:T(2,128)(2,1)}), bf16[4,2,16384]{2,1,0:T(2,128)(2,1)S(1)}, u32[]{:S(2)}, u32[]{:S(2)}) async-start(bf16[4,2,16384]{2,1,0:T(2,128)(2,1)} %reshape.296), calls=%async_computation.9 | async-start | bytes 524288 | tf_op jit(solution)/shard_map/all_to_all | solution.py:106
  143.6 1.1 copy.83
  144.7 5.4 %all-to-all-done.9 = bf16[4,2,16384]{2,1,0:T(2,128)(2,1)S(1)} async-done(((bf16[4,2,16384]{2,1,0:T(2,128)(2,1)}), bf16[4,2,16384]{2,1,0:T(2,128)(2,1)S(1)}, u32[]{:S(2)}, u32[]{:S(2)}) %all-to-all-start.9) | async-done | bytes 262176 | tf_op jit(solution)/shard_map/all_to_all | solution.py:106
  150.1 3.5 %all-to-all-start.8 = ((bf16[256,8,128]{2,1,0:T(8,128)(2,1)}), bf16[256,8,128]{2,1,0:T(8,128)(2,1)S(1)}, u32[]{:S(2)}, u32[]{:S(2)}) async-start(bf16[256,8,128]{2,1,0:T(8,128)(2,1)} %copy.83), calls=%async_computation.8 | async-start | bytes 1048576 | tf_op jit(solution)/shard_map/all_to_all | solution.py:107
  153.9 0.9 copy.89
  154.8 7.6 %all-to-all-done.8 = bf16[256,8,128]{2,1,0:T(8,128)(2,1)S(1)} async-done(((bf16[256,8,128]{2,1,0:T(8,128)(2,1)}), bf16[256,8,128]{2,1,0:T(8,128)(2,1)S(1)}, u32[]{:S(2)}, u32[]{:S(2)}) %all-to-all-start.8) | async-done | bytes 524320 | tf_op jit(solution)/shard_map/all_to_all | solution.py:107
  162.4 3.4 %all-to-all-start.12 = ((bf16[256,4,128]{2,1,0:T(4,128)(2,1)}), bf16[256,4,128]{2,1,0:T(4,128)(2,1)S(1)}, u32[]{:S(2)}, u32[]{:S(2)}) async-start(bf16[256,4,128]{2,1,0:T(4,128)(2,1)} %copy.89), calls=%async_computation.12 | async-start | bytes 524288 | tf_op jit(solution)/shard_map/all_to_all | solution.py:107
  167.1 4.7 %all-to-all-done.12 = bf16[256,4,128]{2,1,0:T(4,128)(2,1)S(1)} async-done(((bf16[256,4,128]{2,1,0:T(4,128)(2,1)}), bf16[256,4,128]{2,1,0:T(4,128)(2,1)S(1)}, u32[]{:S(2)}, u32[]{:S(2)}) %all-to-all-start.12) | async-done | bytes 262176 | tf_op jit(solution)/shard_map/all_to_all | solution.py:107
  171.8 3.4 %all-to-all-start.10 = ((bf16[256,4,128]{2,1,0:T(4,128)(2,1)}), bf16[256,4,128]{2,1,0:T(4,128)(2,1)S(1)}, u32[]{:S(2)}, u32[]{:S(2)}) async-start(bf16[256,4,128]{2,1,0:T(4,128)(2,1)} %copy.86), calls=%async_computation.10 | async-start | bytes 524288 | tf_op jit(solution)/shard_map/all_to_all | solution.py:107
  176.9 4.3 %all-to-all-done.10 = bf16[256,4,128]{2,1,0:T(4,128)(2,1)S(1)} async-done(((bf16[256,4,128]{2,1,0:T(4,128)(2,1)}), bf16[256,4,128]{2,1,0:T(4,128)(2,1)S(1)}, u32[]{:S(2)}, u32[]{:S(2)}) %all-to-all-start.10) | async-done | bytes 262176 | tf_op jit(solution)/shard_map/all_to_all | solution.py:107
  (64 shorter events, 13.6 us)
Async XLA Ops:
  0.6 8.4 %copy-start.8 = (s32[256]{0:T(256)S(1)}, s32[256]{0:T(256)}, u32[]{:S(2)}) copy-start(s32[256]{0:T(256)} %param.29) | copy-start | bytes 3076
  0.6 18.6 %copy-start.6 = (bf16[64,32,128]{2,1,0:T(8,128)(2,1)S(1)}, bf16[64,32,128]{2,1,0:T(8,128)(2,1)}, u32[]{:S(2)}) copy-start(bf16[64,32,128]{2,1,0:T(8,128)(2,1)} %param.27) | copy-start | bytes 1572868
  2.4 18.6 %all-to-all-start = ((bf16[256,4,128]{2,0,1:T(8,128)(2,1)}), bf16[256,4,128]{2,0,1:T(8,128)(2,1)S(1)}, u32[]{:S(2)}, u32[]{:S(2)}) async-start(bf16[256,4,128]{2,0,1:T(8,128)(2,1)} %copy.69), calls=%async_computation | async-start | bytes 524288 | tf_op jit(solution)/shard_map/all_to_all | solution.py:68
  21.0 23.0 %copy-start.4 = (bf16[256,4,128]{2,0,1:T(8,128)(2,1)}, bf16[256,4,128]{2,0,1:T(8,128)(2,1)S(1)}, u32[]{:S(2)}) copy-start(bf16[256,4,128]{2,0,1:T(8,128)(2,1)S(1)} %all-to-all-done) | copy-start | bytes 786436
  21.0 10.8 %all-to-all-start.3 = ((bf16[4,256,1,128]{3,1,2,0:T(8,128)(2,1)}), bf16[4,256,1,128]{3,1,2,0:T(8,128)(2,1)}, u32[]{:S(2)}, u32[]{:S(2)}) async-start(bf16[4,256,1,128]{3,1,2,0:T(8,128)(2,1)} %pad_maximum_fusion.2), calls=%async_computation.3 | async-start | bytes 524288 | tf_op jit(solution)/shard_map/all_to_all | solution.py:72
  25.1 18.9 %copy-start.7 = (f32[8,256]{1,0:T(8,128)S(1)}, f32[8,256]{1,0:T(8,128)}, u32[]{:S(2)}) copy-start(f32[8,256]{1,0:T(8,128)} %param.28) | copy-start | bytes 24580
  31.8 16.6 %all-to-all-start.4 = ((bf16[64,32,128]{2,0,1:T(8,128)(2,1)}), bf16[64,32,128]{2,0,1:T(8,128)(2,1)S(1)}, u32[]{:S(2)}, u32[]{:S(2)}) async-start(bf16[64,32,128]{2,0,1:T(8,128)(2,1)} %copy.75), calls=%async_computation.4 | async-start | bytes 1048576 | tf_op jit(solution)/shard_map/all_to_all | solution.py:61
  37.1 23.3 %collective-permute-start = (bf16[1024,128]{1,0:T(8,128)(2,1)S(1)}, bf16[1024,128]{1,0:T(8,128)(2,1)}, u32[]{:S(2)}, u32[]{:S(2)}) collective-permute-start(bf16[1024,128]{1,0:T(8,128)(2,1)S(1)} %bitcast.172), channel_id=1, source_target_pairs={{0,4},{4,8},{8,12},{12,16},{16,20},{20,24},{24,28},{28,32},{32,36}... | collective-permute-start | bytes 786440 | tf_op jit(solution)/shard_map/ppermute | solution.py:15
  44.6 17.2 %collective-permute-start.1 = (bf16[1024,128]{1,0:T(8,128)(2,1)}, bf16[1024,128]{1,0:T(8,128)(2,1)}, u32[]{:S(2)}, u32[]{:S(2)}) collective-permute-start(bf16[1024,128]{1,0:T(8,128)(2,1)} %bitcast.20), channel_id=1, source_target_pairs={{0,4},{4,8},{8,12},{12,16},{16,20},{20,24},{24,28},{28,32},{32,36}... | collective-permute-start | bytes 786440 | tf_op jit(solution)/shard_map/ppermute | solution.py:15
  48.4 8.5 %all-to-all-start.2 = ((f32[4,2,256]{2,1,0:T(2,128)}), f32[4,2,256]{2,1,0:T(2,128)S(1)}, u32[]{:S(2)}, u32[]{:S(2)}) async-start(f32[4,2,256]{2,1,0:T(2,128)} %all_to_all.153), calls=%async_computation.2 | async-start | bytes 16384 | tf_op jit(solution)/shard_map/all_to_all | solution.py:83
  52.6 7.9 %copy-start.5 = (bf16[256,4,128]{2,0,1:T(8,128)(2,1)S(1)}, bf16[256,4,128]{2,0,1:T(8,128)(2,1)}, u32[]{:S(2)}) copy-start(bf16[256,4,128]{2,0,1:T(8,128)(2,1)} %copy-done.4) | copy-start | bytes 786436
  57.0 12.5 %all-to-all-start.1 = ((bf16[256,8,128]{2,0,1:T(8,128)(2,1)}), bf16[256,8,128]{2,0,1:T(8,128)(2,1)S(1)}, u32[]{:S(2)}, u32[]{:S(2)}) async-start(bf16[256,8,128]{2,0,1:T(8,128)(2,1)} %copy.70), calls=%async_computation.1 | async-start | bytes 1048576 | tf_op jit(solution)/shard_map/all_to_all | solution.py:66
  61.8 17.4 %copy-start = (bf16[1,1280,128]{2,1,0:T(8,128)(2,1)}, bf16[1,1280,128]{2,1,0:T(8,128)(2,1)S(1)}, u32[]{:S(2)}) copy-start(bf16[1,1280,128]{2,1,0:T(8,128)(2,1)S(1)} %get-tuple-element.105) | copy-start | bytes 983044
  61.8 17.4 %copy-start.2 = (bf16[1,1280,128]{2,1,0:T(8,128)(2,1)}, bf16[1,1280,128]{2,1,0:T(8,128)(2,1)S(1)}, u32[]{:S(2)}) copy-start(bf16[1,1280,128]{2,1,0:T(8,128)(2,1)S(1)} %get-tuple-element.106) | copy-start | bytes 983044
  69.5 12.3 %all-to-all-start.5 = ((bf16[256,8,128]{2,0,1:T(8,128)(2,1)}), bf16[256,8,128]{2,0,1:T(8,128)(2,1)}, u32[]{:S(2)}, u32[]{:S(2)}) async-start(bf16[256,8,128]{2,0,1:T(8,128)(2,1)} %bitcast.29), calls=%async_computation.5 | async-start | bytes 1048576 | tf_op jit(solution)/shard_map/all_to_all | solution.py:67
  81.8 17.9 %all-to-all-start.6 = ((f32[4,2,256]{2,1,0:T(2,128)}), f32[4,2,256]{2,1,0:T(2,128)S(1)}, u32[]{:S(2)}, u32[]{:S(2)}) async-start(f32[4,2,256]{2,1,0:T(2,128)} %all_to_all.163), calls=%async_computation.6 | async-start | bytes 16384 | tf_op jit(solution)/shard_map/all_to_all | solution.py:84
  92.0 29.9 %collective-permute-start.3 = (f32[1024,128]{1,0:T(8,128)}, f32[1024,128]{1,0:T(8,128)}, u32[]{:S(2)}, u32[]{:S(2)}) collective-permute-start(f32[1024,128]{1,0:T(8,128)} %slice.261), channel_id=1, source_target_pairs={{4,0},{8,4},{12,8},{16,12},{20,16},{24,20},{28,24},{32,28},{36,32}... | collective-permute-start | bytes 1572872 | tf_op jit(solution)/shard_map/ppermute | solution.py:15
  107.9 4.8 %copy-start.1 = (bf16[1,1280,128]{2,1,0:T(8,128)(2,1)S(1)}, bf16[1,1280,128]{2,1,0:T(8,128)(2,1)}, u32[]{:S(2)}) copy-start(bf16[1,1280,128]{2,1,0:T(8,128)(2,1)} %copy-done) | copy-start | bytes 983044
  107.9 4.8 %copy-start.3 = (bf16[1,1280,128]{2,1,0:T(8,128)(2,1)S(1)}, bf16[1,1280,128]{2,1,0:T(8,128)(2,1)}, u32[]{:S(2)}) copy-start(bf16[1,1280,128]{2,1,0:T(8,128)(2,1)} %copy-done.2) | copy-start | bytes 983044
  108.9 24.5 %collective-permute-start.2 = (f32[1024,128]{1,0:T(8,128)}, f32[1024,128]{1,0:T(8,128)}, u32[]{:S(2)}, u32[]{:S(2)}) collective-permute-start(f32[1024,128]{1,0:T(8,128)} %slice.253), channel_id=1, source_target_pairs={{4,0},{8,4},{12,8},{16,12},{20,16},{24,20},{28,24},{32,28},{36,32}... | collective-permute-start | bytes 1572872 | tf_op jit(solution)/shard_map/ppermute | solution.py:15
  117.2 12.8 %all-to-all-start.7 = ((bf16[1024,2,128]{2,1,0:T(2,128)(2,1)}), bf16[1024,2,128]{2,1,0:T(2,128)(2,1)S(1)}, u32[]{:S(2)}, u32[]{:S(2)}) async-start(bf16[1024,2,128]{2,1,0:T(2,128)(2,1)} %copy.80), calls=%async_computation.7 | async-start | bytes 1048576 | tf_op jit(solution)/shard_map/all_to_all | solution.py:106
  130.0 10.1 %all-to-all-start.11 = ((bf16[4,2,16384]{2,1,0:T(2,128)(2,1)}), bf16[4,2,16384]{2,1,0:T(2,128)(2,1)S(1)}, u32[]{:S(2)}, u32[]{:S(2)}) async-start(bf16[4,2,16384]{2,1,0:T(2,128)(2,1)} %reshape.298), calls=%async_computation.11 | async-start | bytes 524288 | tf_op jit(solution)/shard_map/all_to_all | solution.py:106
  140.0 10.1 %all-to-all-start.9 = ((bf16[4,2,16384]{2,1,0:T(2,128)(2,1)}), bf16[4,2,16384]{2,1,0:T(2,128)(2,1)S(1)}, u32[]{:S(2)}, u32[]{:S(2)}) async-start(bf16[4,2,16384]{2,1,0:T(2,128)(2,1)} %reshape.296), calls=%async_computation.9 | async-start | bytes 524288 | tf_op jit(solution)/shard_map/all_to_all | solution.py:106
  150.1 12.3 %all-to-all-start.8 = ((bf16[256,8,128]{2,1,0:T(8,128)(2,1)}), bf16[256,8,128]{2,1,0:T(8,128)(2,1)S(1)}, u32[]{:S(2)}, u32[]{:S(2)}) async-start(bf16[256,8,128]{2,1,0:T(8,128)(2,1)} %copy.83), calls=%async_computation.8 | async-start | bytes 1048576 | tf_op jit(solution)/shard_map/all_to_all | solution.py:107
  162.4 9.4 %all-to-all-start.12 = ((bf16[256,4,128]{2,1,0:T(4,128)(2,1)}), bf16[256,4,128]{2,1,0:T(4,128)(2,1)S(1)}, u32[]{:S(2)}, u32[]{:S(2)}) async-start(bf16[256,4,128]{2,1,0:T(4,128)(2,1)} %copy.89), calls=%async_computation.12 | async-start | bytes 524288 | tf_op jit(solution)/shard_map/all_to_all | solution.py:107
  171.8 9.4 %all-to-all-start.10 = ((bf16[256,4,128]{2,1,0:T(4,128)(2,1)}), bf16[256,4,128]{2,1,0:T(4,128)(2,1)S(1)}, u32[]{:S(2)}, u32[]{:S(2)}) async-start(bf16[256,4,128]{2,1,0:T(4,128)(2,1)} %copy.86), calls=%async_computation.10 | async-start | bytes 524288 | tf_op jit(solution)/shard_map/all_to_all | solution.py:107
